TPU v7x, 256 devices: a whole 4x4x8 slice. The times are simulated.
256 devices in a mesh: dp: 16 (over z_lo, y, core), expert: 16 (over x, z_hi).
Axes of the slice: x: 4, y: 4, z: 8 (z_hi: 4, z_lo: 2; z = z_hi * 2 + z_lo), core: 2. Of those that a mesh axis runs over, the one named last changes fastest.
Arguments:
- tokens: bfloat16 [32768, 2048], P(('dp', 'expert')), may hold values from -6 to 6
- cotangent: bfloat16 [32768, 2048], P(('dp', 'expert')), may hold values from -6 to 6
- hot_mask: int32 [32768], P(('dp', 'expert')), may hold values 0 or 1
- hot_gate: float32 [32768], P(('dp', 'expert')), may hold values from 0.2 to 1
- cold_ids: int32 [32768, 1], P(('dp', 'expert')), may hold values from 0 to 7; in each aligned block of 128 rows (0 to 127, 128 to 255, ...) at most 20 rows name the same one
- cold_gate: float32 [32768, 1], P(('dp', 'expert')), may hold values from 0.2 to 1
- hot_in: bfloat16 [2, 704, 2048], P(None, 'dp'), may hold values from -0.125 to 0.125
- hot_down: bfloat16 [704, 2048], P('dp'), may hold values from -0.21875 to 0.21875
- cold_in: bfloat16 [2, 5632, 2048], P(None, 'expert'), may hold values from -0.125 to 0.125
- cold_down: bfloat16 [5632, 2048], P('expert'), may hold values from -0.21875 to 0.21875
Outputs:
- mixed: bfloat16 [32768, 2048], P(('dp', 'expert'))
- input_grad: bfloat16 [32768, 2048], P(('dp', 'expert'))
- hot_grad_in: float32 [2, 704, 2048], P(None, 'dp', 'expert')
- hot_grad_down: float32 [704, 2048], P('dp', 'expert')
- cold_grad_in: bfloat16 [16, 2, 5632, 2048], P('dp', None, 'expert')
- cold_grad_down: bfloat16 [16, 5632, 2048], P('dp', 'expert')
Inputs may be any that keep to these rules, and one draw needn't show every extreme that they name: `cold_ids`: in each device's block of 128 rows no cold expert is chosen by more than 20 rows, and in every draw some device's block chooses some cold expert exactly 20 times.
All inputs are finite; a program needn't handle non-finite values. No bound on the sum of `hot_mask` on one device may be relied on, other than what follows from the above.
Results may differ from a plain program's by a relative error of at most 0.0059.
Values may be sent and summed in bfloat16 or wider, within the bound.
No kernel may reach another device: no remote copies, remote signals or barrier semaphores. Data moves between devices by JAX's collectives and lax.ppermute only.
A program may use at most 128 MiB of HBM per device.

v0:
```python
import math
import jax
import jax.numpy as jnp
from jax import lax
from jax.sharding import PartitionSpec as P


def passed_along(block, axis, distance):
    devices = range(lax.axis_size(axis))
    route = [((i - distance) % len(devices), i) for i in devices]
    return lax.ppermute(block, axis, route)


def silu_parts(values):
    sigmoid_val = jax.nn.sigmoid(values)
    return (values * sigmoid_val, sigmoid_val * (1.0 + values * (1.0 - sigmoid_val)))


def pass_weights(weights):
    return passed_along(weights, "dp", 1)


def pass_grads(carried):
    return passed_along(carried, "dp", 1)


def hot_terms(tokens, cotangent, hot_weight, weights):
    pre_act = jnp.einsum("td,kud->ktu", tokens, weights[:2], preferred_element_type=jnp.float32)
    silu_out, silu_slope = silu_parts(pre_act[0])
    hidden = (hot_weight[:, None] * silu_out * pre_act[1]).astype(jnp.bfloat16)
    out_part = jnp.dot(hidden, weights[2], preferred_element_type=jnp.float32)
    back_proj = jnp.einsum("td,ud->tu", cotangent, weights[2], preferred_element_type=jnp.float32)
    hidden_grad = hot_weight[:, None] * back_proj
    pre_grad = jnp.stack([hidden_grad * pre_act[1] * silu_slope, hidden_grad * silu_out]).astype(
        jnp.bfloat16
    )
    dx_part = jnp.einsum("ktu,kud->td", pre_grad, weights[:2], preferred_element_type=jnp.float32)
    grad_in = jnp.einsum("ktu,td->kud", pre_grad, tokens, preferred_element_type=jnp.float32)
    grad_down = jnp.einsum("tu,td->ud", hidden, cotangent, preferred_element_type=jnp.float32)
    return (out_part, dx_part, jnp.concatenate([grad_in, grad_down[None]], axis=0))


def cold_terms(row_block, cold_in, cold_down):
    pre_act = jnp.einsum("rd,kud->kru", row_block[0], cold_in, preferred_element_type=jnp.float32)
    silu_out, silu_slope = silu_parts(pre_act[0])
    hidden = (silu_out * pre_act[1]).astype(jnp.bfloat16)
    out_part = jnp.dot(hidden, cold_down, preferred_element_type=jnp.float32).astype(jnp.bfloat16)
    back_proj = jnp.einsum("rd,ud->ru", row_block[1], cold_down, preferred_element_type=jnp.float32)
    pre_grad = jnp.stack([back_proj * pre_act[1] * silu_slope, back_proj * silu_out]).astype(
        jnp.bfloat16
    )
    dx_part = jnp.einsum(
        "kru,kud->rd", pre_grad, cold_in, preferred_element_type=jnp.float32
    ).astype(jnp.bfloat16)
    grad_in = jnp.einsum("kru,rd->kud", pre_grad, row_block[0], preferred_element_type=jnp.float32)
    grad_down = jnp.einsum("ru,rd->ud", hidden, row_block[1], preferred_element_type=jnp.float32)
    return (out_part, dx_part, grad_in, grad_down)


def body(
    tokens, cotangent, hot_mask, hot_gate, cold_ids, cold_gate, hot_in, hot_down, cold_in, cold_down
):
    tok_dev, model_width = tokens.shape
    top_cold = cold_ids.shape[1]
    data_count = lax.axis_size("dp")
    owner_count = lax.axis_size("expert")
    cold_count = owner_count // 2
    capacity = 5 * tok_dev * top_cold // (4 * cold_count)
    hot_weight = hot_mask.astype(jnp.float32) * hot_gate
    hot_stack = jnp.concatenate([hot_in, hot_down[None]], axis=0)
    ids_flat = cold_ids.reshape(-1)
    one_hot = (ids_flat[:, None] == jnp.arange(cold_count, dtype=jnp.int32)[None, :]).astype(
        jnp.int32
    )
    earlier = jnp.cumsum(one_hot, axis=0) - one_hot
    slot_pos = jnp.sum(one_hot * earlier, axis=1)
    column = ids_flat * capacity + slot_pos
    dispatch = (
        column[:, None] == jnp.arange(cold_count * capacity, dtype=jnp.int32)[None, :]
    ).astype(jnp.bfloat16)
    gates_flat = cold_gate.reshape(-1)
    row_tok = jnp.repeat(tokens, top_cold, axis=0)
    row_cot = (gates_flat[:, None] * jnp.repeat(cotangent, top_cold, axis=0)).astype(jnp.bfloat16)
    stacked = jnp.stack([row_tok, row_cot])
    send_rows = jnp.einsum(
        "rc,srd->scd", dispatch, stacked, preferred_element_type=jnp.float32
    ).astype(jnp.bfloat16)
    send_rows = send_rows.reshape(2, cold_count, capacity, model_width)
    duplicate = jnp.broadcast_to(
        send_rows[:, :, None], (2, cold_count, 2, capacity, model_width)
    ).reshape(2, owner_count, capacity, model_width)
    received = lax.all_to_all(duplicate, "expert", split_axis=1, concat_axis=1, tiled=True)
    row_block = received.reshape(2, owner_count * capacity, model_width)
    out_part, dx_part, cold_grad_in, cold_grad_down = cold_terms(row_block, cold_in, cold_down)
    returned = lax.all_to_all(
        jnp.stack([out_part, dx_part]).reshape(2, owner_count, capacity, model_width),
        "expert",
        split_axis=1,
        concat_axis=1,
        tiled=True,
    )
    summed = jnp.sum(
        returned.astype(jnp.float32).reshape(2, cold_count, 2, capacity, model_width), axis=2
    )
    summed = summed.reshape(2, cold_count * capacity, model_width)
    picked = jnp.take(summed, column, axis=1)
    cold_out = jnp.sum(
        gates_flat.reshape(tok_dev, top_cold, 1)
        * picked[0].reshape(tok_dev, top_cold, model_width),
        axis=1,
    )
    cold_dx = jnp.sum(picked[1].reshape(tok_dev, top_cold, model_width), axis=1)
    own_terms = hot_terms(tokens, cotangent, hot_weight, hot_stack)
    weights = pass_weights(hot_stack)
    first_terms = hot_terms(tokens, cotangent, hot_weight, weights)

    def cycle_turn(hop_count, cycle_state):
        weights, carried, out_sum, dx_sum = cycle_state
        weights = pass_weights(weights)
        carried = pass_grads(carried)
        fresh_terms = hot_terms(tokens, cotangent, hot_weight, weights)
        return (
            weights,
            carried + fresh_terms[2],
            out_sum + fresh_terms[0],
            dx_sum + fresh_terms[1],
        )

    cycle_state = (
        weights,
        first_terms[2],
        own_terms[0] + first_terms[0],
        own_terms[1] + first_terms[1],
    )
    weights, carried, hot_out, hot_dx = lax.fori_loop(2, data_count, cycle_turn, cycle_state)
    hot_grads = pass_grads(carried) + own_terms[2]
    scale_hot = 1.0 / math.sqrt(tok_dev * data_count * owner_count)
    hot_cols = lax.psum_scatter(hot_grads, "expert", scatter_dimension=2, tiled=True) * scale_hot
    scale_cold = 1.0 / math.sqrt(tok_dev * owner_count)
    mixed = (hot_out + cold_out).astype(jnp.bfloat16)
    input_grad = (hot_dx + cold_dx).astype(jnp.bfloat16)
    return (
        mixed,
        input_grad,
        hot_cols[:2],
        hot_cols[2],
        (cold_grad_in * scale_cold).astype(jnp.bfloat16)[None],
        (cold_grad_down * scale_cold).astype(jnp.bfloat16)[None],
    )


def solution(mesh):
    return jax.shard_map(
        body,
        mesh=mesh,
        in_specs=(
            P(("dp", "expert"), None),
            P(("dp", "expert"), None),
            P(("dp", "expert")),
            P(("dp", "expert")),
            P(("dp", "expert"), None),
            P(("dp", "expert"), None),
            P(None, "dp", None),
            P("dp", None),
            P(None, "expert", None),
            P("expert", None),
        ),
        out_specs=(
            P(("dp", "expert"), None),
            P(("dp", "expert"), None),
            P(None, "dp", "expert"),
            P("dp", "expert"),
            P("dp", None, "expert", None),
            P("dp", "expert", None),
        ),
        check_vma=False,
    )
```

profile of v0, /device:TPU:8, one launch (start us, length us, event | category | flops | bytes accessed | tf_op | source)
XLA Modules:
  0.0 713.6 jit_solution(3561489298241170776)
XLA Ops:
  16.4 11.1 %all-to-all-start = ((bf16[2,16,20,2048]{3,0,2,1:T(2,128)(2,1)}), bf16[2,16,20,2048]{3,0,2,1:T(2,128)(2,1)}, u32[]{:S(2)}, u32[]{:S(2)}) async-start(bf16[2,16,20,2048]{3,0,2,1:T(2,128)(2,1)} %bitcast.326), calls=%async_computation | async-start | bytes 5242880 | tf_op jit(solution)/shard_map/all_to_all | solution.py:92
  31.1 8.0 %collective-permute-done.2 = bf16[3,44,2048]{2,1,0:T(8,128)(2,1)S(1)} collective-permute-done((bf16[3,44,2048]{2,1,0:T(8,128)(2,1)S(1)}, bf16[3,44,2048]{2,1,0:T(8,128)(2,1)S(1)}, u32[]{:S(2)}, u32[]{:S(2)}) %collective-permute-start.2) | collective-permute-done | bytes 540704 | tf_op jit(solution)/shard_map/ppermute | solution.py:11
  44.0 47.6 %all-to-all-done = bf16[2,16,20,2048]{3,0,2,1:T(2,128)(2,1)} async-done(((bf16[2,16,20,2048]{3,0,2,1:T(2,128)(2,1)}), bf16[2,16,20,2048]{3,0,2,1:T(2,128)(2,1)}, u32[]{:S(2)}, u32[]{:S(2)}) %all-to-all-start) | async-done | bytes 2621472 | tf_op jit(solution)/shard_map/all_to_all | solution.py:92
  91.6 14.8 %slice_reduce_fusion.1 = (bf16[16,20,2048]{2,1,0:T(8,128)(2,1)}, bf16[16,20,2048]{2,1,0:T(8,128)(2,1)}) fusion(bf16[2,16,20,2048]{3,0,2,1:T(2,128)(2,1)} %all-to-all-done), kind=kLoop, calls=%fused_computation.49 | loop fusion | bytes 5242880 | tf_op jit(solution)/shard_map/slice | solution.py:44
  140.0 414.7 %while.16 = (s32[]{:T(128)}, bf16[3,44,2048]{2,1,0:T(8,128)(2,1)}, f32[3,44,2048]{2,1,0:T(8,128)}, f32[128,2048]{1,0:T(8,128)}, f32[128,2048]{1,0:T(8,128)}, /*i...) while((s32[]{:T(128)}, bf16[3,44,2048]{2,1,0:T(8,128)(2,1)}, ...), condition=%wide.region_1.2_spmd, body=%wide.region_0.0_spmd.sunk | while | flops 208863232 | bytes 40744796 | solution.py:135
  191.6 50.5 %collective-permute-done = bf16[3,44,2048]{2,1,0:T(8,128)(2,1)S(1)} collective-permute-done((bf16[3,44,2048]{2,1,0:T(8,128)(2,1)}, bf16[3,44,2048]{2,1,0:T(8,128)(2,1)S(1)}, u32[]{:S(2)}, u32[]{:S(2)}) %collective-permute-start) | collective-permute-done | bytes 540704 | tf_op jit(solution)/shard_map/while/body/eval_jaxpr/ppermute | solution.py:11
  247.0 7.9 %collective-permute-done.1 = f32[3,44,2048]{2,1,0:T(8,128)} collective-permute-done((f32[3,44,2048]{2,1,0:T(8,128)}, f32[3,44,2048]{2,1,0:T(8,128)}, u32[]{:S(2)}, u32[]{:S(2)}) %collective-permute-start.1) | collective-permute-done | bytes 1081376 | tf_op jit(solution)/shard_map/while/body/eval_jaxpr/ppermute | solution.py:11
  258.4 10.7 %collective-permute-done = bf16[3,44,2048]{2,1,0:T(8,128)(2,1)S(1)} collective-permute-done((bf16[3,44,2048]{2,1,0:T(8,128)(2,1)}, bf16[3,44,2048]{2,1,0:T(8,128)(2,1)S(1)}, u32[]{:S(2)}, u32[]{:S(2)}) %collective-permute-start) | collective-permute-done | bytes 540704 | tf_op jit(solution)/shard_map/while/body/eval_jaxpr/ppermute | solution.py:11
  274.0 7.9 %collective-permute-done.1 = f32[3,44,2048]{2,1,0:T(8,128)} collective-permute-done((f32[3,44,2048]{2,1,0:T(8,128)}, f32[3,44,2048]{2,1,0:T(8,128)}, u32[]{:S(2)}, u32[]{:S(2)}) %collective-permute-start.1) | collective-permute-done | bytes 1081376 | tf_op jit(solution)/shard_map/while/body/eval_jaxpr/ppermute | solution.py:11
  285.4 10.7 %collective-permute-done = bf16[3,44,2048]{2,1,0:T(8,128)(2,1)S(1)} collective-permute-done((bf16[3,44,2048]{2,1,0:T(8,128)(2,1)}, bf16[3,44,2048]{2,1,0:T(8,128)(2,1)S(1)}, u32[]{:S(2)}, u32[]{:S(2)}) %collective-permute-start) | collective-permute-done | bytes 540704 | tf_op jit(solution)/shard_map/while/body/eval_jaxpr/ppermute | solution.py:11
  301.0 7.9 %collective-permute-done.1 = f32[3,44,2048]{2,1,0:T(8,128)} collective-permute-done((f32[3,44,2048]{2,1,0:T(8,128)}, f32[3,44,2048]{2,1,0:T(8,128)}, u32[]{:S(2)}, u32[]{:S(2)}) %collective-permute-start.1) | collective-permute-done | bytes 1081376 | tf_op jit(solution)/shard_map/while/body/eval_jaxpr/ppermute | solution.py:11
  312.5 10.7 %collective-permute-done = bf16[3,44,2048]{2,1,0:T(8,128)(2,1)S(1)} collective-permute-done((bf16[3,44,2048]{2,1,0:T(8,128)(2,1)}, bf16[3,44,2048]{2,1,0:T(8,128)(2,1)S(1)}, u32[]{:S(2)}, u32[]{:S(2)}) %collective-permute-start) | collective-permute-done | bytes 540704 | tf_op jit(solution)/shard_map/while/body/eval_jaxpr/ppermute | solution.py:11
  339.5 10.7 %collective-permute-done = bf16[3,44,2048]{2,1,0:T(8,128)(2,1)S(1)} collective-permute-done((bf16[3,44,2048]{2,1,0:T(8,128)(2,1)}, bf16[3,44,2048]{2,1,0:T(8,128)(2,1)S(1)}, u32[]{:S(2)}, u32[]{:S(2)}) %collective-permute-start) | collective-permute-done | bytes 540704 | tf_op jit(solution)/shard_map/while/body/eval_jaxpr/ppermute | solution.py:11
  366.5 10.7 %collective-permute-done = bf16[3,44,2048]{2,1,0:T(8,128)(2,1)S(1)} collective-permute-done((bf16[3,44,2048]{2,1,0:T(8,128)(2,1)}, bf16[3,44,2048]{2,1,0:T(8,128)(2,1)S(1)}, u32[]{:S(2)}, u32[]{:S(2)}) %collective-permute-start) | collective-permute-done | bytes 540704 | tf_op jit(solution)/shard_map/while/body/eval_jaxpr/ppermute | solution.py:11
  393.5 10.7 %collective-permute-done = bf16[3,44,2048]{2,1,0:T(8,128)(2,1)S(1)} collective-permute-done((bf16[3,44,2048]{2,1,0:T(8,128)(2,1)}, bf16[3,44,2048]{2,1,0:T(8,128)(2,1)S(1)}, u32[]{:S(2)}, u32[]{:S(2)}) %collective-permute-start) | collective-permute-done | bytes 540704 | tf_op jit(solution)/shard_map/while/body/eval_jaxpr/ppermute | solution.py:11
  420.5 10.7 %collective-permute-done = bf16[3,44,2048]{2,1,0:T(8,128)(2,1)S(1)} collective-permute-done((bf16[3,44,2048]{2,1,0:T(8,128)(2,1)}, bf16[3,44,2048]{2,1,0:T(8,128)(2,1)S(1)}, u32[]{:S(2)}, u32[]{:S(2)}) %collective-permute-start) | collective-permute-done | bytes 540704 | tf_op jit(solution)/shard_map/while/body/eval_jaxpr/ppermute | solution.py:11
  447.6 10.7 %collective-permute-done = bf16[3,44,2048]{2,1,0:T(8,128)(2,1)S(1)} collective-permute-done((bf16[3,44,2048]{2,1,0:T(8,128)(2,1)}, bf16[3,44,2048]{2,1,0:T(8,128)(2,1)S(1)}, u32[]{:S(2)}, u32[]{:S(2)}) %collective-permute-start) | collective-permute-done | bytes 540704 | tf_op jit(solution)/shard_map/while/body/eval_jaxpr/ppermute | solution.py:11
  463.2 7.9 %collective-permute-done.1 = f32[3,44,2048]{2,1,0:T(8,128)} collective-permute-done((f32[3,44,2048]{2,1,0:T(8,128)}, f32[3,44,2048]{2,1,0:T(8,128)}, u32[]{:S(2)}, u32[]{:S(2)}) %collective-permute-start.1) | collective-permute-done | bytes 1081376 | tf_op jit(solution)/shard_map/while/body/eval_jaxpr/ppermute | solution.py:11
  474.6 10.7 %collective-permute-done = bf16[3,44,2048]{2,1,0:T(8,128)(2,1)S(1)} collective-permute-done((bf16[3,44,2048]{2,1,0:T(8,128)(2,1)}, bf16[3,44,2048]{2,1,0:T(8,128)(2,1)S(1)}, u32[]{:S(2)}, u32[]{:S(2)}) %collective-permute-start) | collective-permute-done | bytes 540704 | tf_op jit(solution)/shard_map/while/body/eval_jaxpr/ppermute | solution.py:11
  490.2 7.9 %collective-permute-done.1 = f32[3,44,2048]{2,1,0:T(8,128)} collective-permute-done((f32[3,44,2048]{2,1,0:T(8,128)}, f32[3,44,2048]{2,1,0:T(8,128)}, u32[]{:S(2)}, u32[]{:S(2)}) %collective-permute-start.1) | collective-permute-done | bytes 1081376 | tf_op jit(solution)/shard_map/while/body/eval_jaxpr/ppermute | solution.py:11
  501.6 10.7 %collective-permute-done = bf16[3,44,2048]{2,1,0:T(8,128)(2,1)S(1)} collective-permute-done((bf16[3,44,2048]{2,1,0:T(8,128)(2,1)}, bf16[3,44,2048]{2,1,0:T(8,128)(2,1)S(1)}, u32[]{:S(2)}, u32[]{:S(2)}) %collective-permute-start) | collective-permute-done | bytes 540704 | tf_op jit(solution)/shard_map/while/body/eval_jaxpr/ppermute | solution.py:11
  528.6 10.7 %collective-permute-done = bf16[3,44,2048]{2,1,0:T(8,128)(2,1)S(1)} collective-permute-done((bf16[3,44,2048]{2,1,0:T(8,128)(2,1)}, bf16[3,44,2048]{2,1,0:T(8,128)(2,1)S(1)}, u32[]{:S(2)}, u32[]{:S(2)}) %collective-permute-start) | collective-permute-done | bytes 540704 | tf_op jit(solution)/shard_map/while/body/eval_jaxpr/ppermute | solution.py:11
  556.5 16.4 %collective-permute-done.3 = f32[3,44,2048]{2,1,0:T(8,128)S(1)} collective-permute-done((f32[3,44,2048]{2,1,0:T(8,128)}, f32[3,44,2048]{2,1,0:T(8,128)S(1)}, u32[]{:S(2)}, u32[]{:S(2)}) %collective-permute-start.3) | collective-permute-done | bytes 1081376 | tf_op jit(solution)/shard_map/ppermute | solution.py:11
  574.2 105.6 %reduce-scatter.2.cloned.1.call-done = f32[3,44,128]{2,1,0:T(8,128)} async-done(((f32[3,44,2048]{2,1,0:T(8,128)}), f32[3,44,128]{2,1,0:T(8,128)}) %reduce-scatter.2.cloned.1.call-update) | async-done | bytes 67600 | tf_op jit(solution)/shard_map/reduce_scatter | solution.py:138
  (408 shorter events, 286.1 us)
Async XLA Ops:
  16.4 75.2 %all-to-all-start = ((bf16[2,16,20,2048]{3,0,2,1:T(2,128)(2,1)}), bf16[2,16,20,2048]{3,0,2,1:T(2,128)(2,1)}, u32[]{:S(2)}, u32[]{:S(2)}) async-start(bf16[2,16,20,2048]{3,0,2,1:T(2,128)(2,1)} %bitcast.326), calls=%async_computation | async-start | bytes 5242880 | tf_op jit(solution)/shard_map/all_to_all | solution.py:92
  135.5 553.6 %all-to-all-start.1 = ((bf16[2,16,20,2048]{3,0,2,1:T(2,128)(2,1)}), bf16[2,16,20,2048]{3,0,2,1:T(2,128)(2,1)}, u32[]{:S(2)}, u32[]{:S(2)}) async-start(bf16[2,16,20,2048]{3,0,2,1:T(2,128)(2,1)} %copy.31), calls=%async_computation.1 | async-start | bytes 5242880 | tf_op jit(solution)/shard_map/all_to_all | solution.py:95
  139.9 539.8 %reduce-scatter.2.cloned.1.call-start = ((), (), s32[]{:S(2)}) async-start(), calls=%async_computation.3 | async-start | bytes 1253376 | tf_op jit(solution)/shard_map/reduce_scatter | solution.py:138
  140.1 22.3 %collective-permute-start.1 = (f32[3,44,2048]{2,1,0:T(8,128)}, f32[3,44,2048]{2,1,0:T(8,128)}, u32[]{:S(2)}, u32[]{:S(2)}) collective-permute-start(f32[3,44,2048]{2,1,0:T(8,128)} %get-tuple-element.166), channel_id=1, source_target_pairs={{240,0},{0,16},{16,32},{32,48},{48,64},{64,80},{80,96},{96,112},{1... | collective-permute-start | bytes 3244040 | tf_op jit(solution)/shard_map/while/body/eval_jaxpr/ppermute | solution.py:11
  165.0 22.3 %collective-permute-start.1 = (f32[3,44,2048]{2,1,0:T(8,128)}, f32[3,44,2048]{2,1,0:T(8,128)}, u32[]{:S(2)}, u32[]{:S(2)}) collective-permute-start(f32[3,44,2048]{2,1,0:T(8,128)} %get-tuple-element.166), channel_id=1, source_target_pairs={{240,0},{0,16},{16,32},{32,48},{48,64},{64,80},{80,96},{96,112},{1... | collective-permute-start | bytes 3244040 | tf_op jit(solution)/shard_map/while/body/eval_jaxpr/ppermute | solution.py:11
  189.8 52.3 %collective-permute-start = (bf16[3,44,2048]{2,1,0:T(8,128)(2,1)}, bf16[3,44,2048]{2,1,0:T(8,128)(2,1)S(1)}, u32[]{:S(2)}, u32[]{:S(2)}) collective-permute-start(bf16[3,44,2048]{2,1,0:T(8,128)(2,1)} %get-tuple-element.165), channel_id=1, source_target_pairs={{240,0},{0,16},{16,32},{32,48},{48,64},{64,80},{80,96},{96,112},{1... | collective-permute-start | bytes 1622024 | tf_op jit(solution)/shard_map/while/body/eval_jaxpr/ppermute | solution.py:11
  189.9 64.9 %collective-permute-start.1 = (f32[3,44,2048]{2,1,0:T(8,128)}, f32[3,44,2048]{2,1,0:T(8,128)}, u32[]{:S(2)}, u32[]{:S(2)}) collective-permute-start(f32[3,44,2048]{2,1,0:T(8,128)} %get-tuple-element.166), channel_id=1, source_target_pairs={{240,0},{0,16},{16,32},{32,48},{48,64},{64,80},{80,96},{96,112},{1... | collective-permute-start | bytes 3244040 | tf_op jit(solution)/shard_map/while/body/eval_jaxpr/ppermute | solution.py:11
  257.4 11.7 %collective-permute-start = (bf16[3,44,2048]{2,1,0:T(8,128)(2,1)}, bf16[3,44,2048]{2,1,0:T(8,128)(2,1)S(1)}, u32[]{:S(2)}, u32[]{:S(2)}) collective-permute-start(bf16[3,44,2048]{2,1,0:T(8,128)(2,1)} %get-tuple-element.165), channel_id=1, source_target_pairs={{240,0},{0,16},{16,32},{32,48},{48,64},{64,80},{80,96},{96,112},{1... | collective-permute-start | bytes 1622024 | tf_op jit(solution)/shard_map/while/body/eval_jaxpr/ppermute | solution.py:11
  257.5 24.4 %collective-permute-start.1 = (f32[3,44,2048]{2,1,0:T(8,128)}, f32[3,44,2048]{2,1,0:T(8,128)}, u32[]{:S(2)}, u32[]{:S(2)}) collective-permute-start(f32[3,44,2048]{2,1,0:T(8,128)} %get-tuple-element.166), channel_id=1, source_target_pairs={{240,0},{0,16},{16,32},{32,48},{48,64},{64,80},{80,96},{96,112},{1... | collective-permute-start | bytes 3244040 | tf_op jit(solution)/shard_map/while/body/eval_jaxpr/ppermute | solution.py:11
  284.5 24.4 %collective-permute-start.1 = (f32[3,44,2048]{2,1,0:T(8,128)}, f32[3,44,2048]{2,1,0:T(8,128)}, u32[]{:S(2)}, u32[]{:S(2)}) collective-permute-start(f32[3,44,2048]{2,1,0:T(8,128)} %get-tuple-element.166), channel_id=1, source_target_pairs={{240,0},{0,16},{16,32},{32,48},{48,64},{64,80},{80,96},{96,112},{1... | collective-permute-start | bytes 3244040 | tf_op jit(solution)/shard_map/while/body/eval_jaxpr/ppermute | solution.py:11
  311.6 24.4 %collective-permute-start.1 = (f32[3,44,2048]{2,1,0:T(8,128)}, f32[3,44,2048]{2,1,0:T(8,128)}, u32[]{:S(2)}, u32[]{:S(2)}) collective-permute-start(f32[3,44,2048]{2,1,0:T(8,128)} %get-tuple-element.166), channel_id=1, source_target_pairs={{240,0},{0,16},{16,32},{32,48},{48,64},{64,80},{80,96},{96,112},{1... | collective-permute-start | bytes 3244040 | tf_op jit(solution)/shard_map/while/body/eval_jaxpr/ppermute | solution.py:11
  338.6 24.4 %collective-permute-start.1 = (f32[3,44,2048]{2,1,0:T(8,128)}, f32[3,44,2048]{2,1,0:T(8,128)}, u32[]{:S(2)}, u32[]{:S(2)}) collective-permute-start(f32[3,44,2048]{2,1,0:T(8,128)} %get-tuple-element.166), channel_id=1, source_target_pairs={{240,0},{0,16},{16,32},{32,48},{48,64},{64,80},{80,96},{96,112},{1... | collective-permute-start | bytes 3244040 | tf_op jit(solution)/shard_map/while/body/eval_jaxpr/ppermute | solution.py:11
  365.6 24.4 %collective-permute-start.1 = (f32[3,44,2048]{2,1,0:T(8,128)}, f32[3,44,2048]{2,1,0:T(8,128)}, u32[]{:S(2)}, u32[]{:S(2)}) collective-permute-start(f32[3,44,2048]{2,1,0:T(8,128)} %get-tuple-element.166), channel_id=1, source_target_pairs={{240,0},{0,16},{16,32},{32,48},{48,64},{64,80},{80,96},{96,112},{1... | collective-permute-start | bytes 3244040 | tf_op jit(solution)/shard_map/while/body/eval_jaxpr/ppermute | solution.py:11
  392.6 24.4 %collective-permute-start.1 = (f32[3,44,2048]{2,1,0:T(8,128)}, f32[3,44,2048]{2,1,0:T(8,128)}, u32[]{:S(2)}, u32[]{:S(2)}) collective-permute-start(f32[3,44,2048]{2,1,0:T(8,128)} %get-tuple-element.166), channel_id=1, source_target_pairs={{240,0},{0,16},{16,32},{32,48},{48,64},{64,80},{80,96},{96,112},{1... | collective-permute-start | bytes 3244040 | tf_op jit(solution)/shard_map/while/body/eval_jaxpr/ppermute | solution.py:11
  419.6 11.7 %collective-permute-start = (bf16[3,44,2048]{2,1,0:T(8,128)(2,1)}, bf16[3,44,2048]{2,1,0:T(8,128)(2,1)S(1)}, u32[]{:S(2)}, u32[]{:S(2)}) collective-permute-start(bf16[3,44,2048]{2,1,0:T(8,128)(2,1)} %get-tuple-element.165), channel_id=1, source_target_pairs={{240,0},{0,16},{16,32},{32,48},{48,64},{64,80},{80,96},{96,112},{1... | collective-permute-start | bytes 1622024 | tf_op jit(solution)/shard_map/while/body/eval_jaxpr/ppermute | solution.py:11
  419.7 24.4 %collective-permute-start.1 = (f32[3,44,2048]{2,1,0:T(8,128)}, f32[3,44,2048]{2,1,0:T(8,128)}, u32[]{:S(2)}, u32[]{:S(2)}) collective-permute-start(f32[3,44,2048]{2,1,0:T(8,128)} %get-tuple-element.166), channel_id=1, source_target_pairs={{240,0},{0,16},{16,32},{32,48},{48,64},{64,80},{80,96},{96,112},{1... | collective-permute-start | bytes 3244040 | tf_op jit(solution)/shard_map/while/body/eval_jaxpr/ppermute | solution.py:11
  446.6 11.7 %collective-permute-start = (bf16[3,44,2048]{2,1,0:T(8,128)(2,1)}, bf16[3,44,2048]{2,1,0:T(8,128)(2,1)S(1)}, u32[]{:S(2)}, u32[]{:S(2)}) collective-permute-start(bf16[3,44,2048]{2,1,0:T(8,128)(2,1)} %get-tuple-element.165), channel_id=1, source_target_pairs={{240,0},{0,16},{16,32},{32,48},{48,64},{64,80},{80,96},{96,112},{1... | collective-permute-start | bytes 1622024 | tf_op jit(solution)/shard_map/while/body/eval_jaxpr/ppermute | solution.py:11
  446.7 24.4 %collective-permute-start.1 = (f32[3,44,2048]{2,1,0:T(8,128)}, f32[3,44,2048]{2,1,0:T(8,128)}, u32[]{:S(2)}, u32[]{:S(2)}) collective-permute-start(f32[3,44,2048]{2,1,0:T(8,128)} %get-tuple-element.166), channel_id=1, source_target_pairs={{240,0},{0,16},{16,32},{32,48},{48,64},{64,80},{80,96},{96,112},{1... | collective-permute-start | bytes 3244040 | tf_op jit(solution)/shard_map/while/body/eval_jaxpr/ppermute | solution.py:11
  473.6 11.7 %collective-permute-start = (bf16[3,44,2048]{2,1,0:T(8,128)(2,1)}, bf16[3,44,2048]{2,1,0:T(8,128)(2,1)S(1)}, u32[]{:S(2)}, u32[]{:S(2)}) collective-permute-start(bf16[3,44,2048]{2,1,0:T(8,128)(2,1)} %get-tuple-element.165), channel_id=1, source_target_pairs={{240,0},{0,16},{16,32},{32,48},{48,64},{64,80},{80,96},{96,112},{1... | collective-permute-start | bytes 1622024 | tf_op jit(solution)/shard_map/while/body/eval_jaxpr/ppermute | solution.py:11
  473.7 24.4 %collective-permute-start.1 = (f32[3,44,2048]{2,1,0:T(8,128)}, f32[3,44,2048]{2,1,0:T(8,128)}, u32[]{:S(2)}, u32[]{:S(2)}) collective-permute-start(f32[3,44,2048]{2,1,0:T(8,128)} %get-tuple-element.166), channel_id=1, source_target_pairs={{240,0},{0,16},{16,32},{32,48},{48,64},{64,80},{80,96},{96,112},{1... | collective-permute-start | bytes 3244040 | tf_op jit(solution)/shard_map/while/body/eval_jaxpr/ppermute | solution.py:11
  500.6 11.7 %collective-permute-start = (bf16[3,44,2048]{2,1,0:T(8,128)(2,1)}, bf16[3,44,2048]{2,1,0:T(8,128)(2,1)S(1)}, u32[]{:S(2)}, u32[]{:S(2)}) collective-permute-start(bf16[3,44,2048]{2,1,0:T(8,128)(2,1)} %get-tuple-element.165), channel_id=1, source_target_pairs={{240,0},{0,16},{16,32},{32,48},{48,64},{64,80},{80,96},{96,112},{1... | collective-permute-start | bytes 1622024 | tf_op jit(solution)/shard_map/while/body/eval_jaxpr/ppermute | solution.py:11
  500.7 24.4 %collective-permute-start.1 = (f32[3,44,2048]{2,1,0:T(8,128)}, f32[3,44,2048]{2,1,0:T(8,128)}, u32[]{:S(2)}, u32[]{:S(2)}) collective-permute-start(f32[3,44,2048]{2,1,0:T(8,128)} %get-tuple-element.166), channel_id=1, source_target_pairs={{240,0},{0,16},{16,32},{32,48},{48,64},{64,80},{80,96},{96,112},{1... | collective-permute-start | bytes 3244040 | tf_op jit(solution)/shard_map/while/body/eval_jaxpr/ppermute | solution.py:11
  527.7 24.4 %collective-permute-start.1 = (f32[3,44,2048]{2,1,0:T(8,128)}, f32[3,44,2048]{2,1,0:T(8,128)}, u32[]{:S(2)}, u32[]{:S(2)}) collective-permute-start(f32[3,44,2048]{2,1,0:T(8,128)} %get-tuple-element.166), channel_id=1, source_target_pairs={{240,0},{0,16},{16,32},{32,48},{48,64},{64,80},{80,96},{96,112},{1... | collective-permute-start | bytes 3244040 | tf_op jit(solution)/shard_map/while/body/eval_jaxpr/ppermute | solution.py:11
  554.7 18.2 %collective-permute-start.3 = (f32[3,44,2048]{2,1,0:T(8,128)}, f32[3,44,2048]{2,1,0:T(8,128)S(1)}, u32[]{:S(2)}, u32[]{:S(2)}) collective-permute-start(f32[3,44,2048]{2,1,0:T(8,128)} %get-tuple-element.186), channel_id=1, source_target_pairs={{240,0},{0,16},{16,32},{32,48},{48,64},{64,80},{80,96},{96,112},{1... | collective-permute-start | bytes 3244040 | tf_op jit(solution)/shard_map/ppermute | solution.py:11
  (111 other events, 980.1 us)
Sparse Core Ops, SparseCore 0:
  574.2 105.4 reduce-scatter.1
where the time goes:
time: 716 us; the launch traced here: 714 us
  waiting for transfers between devices  472 us (66%)
  matrix products  78.6 us (11%)
  other arithmetic  57.8 us (8%)
  local copies, waits for them, and re-layouts  57 us (8%)
  starting transfers between devices  32 us (4%)
  between operations  14.4 us (2%)
    ppermute x30, waiting for transfers between devices, passed_along(): return lax.ppermute(block, axis, route)  319 us
    reduce_scatter x1, waiting for transfers between devices, body(): lax.psum_scatter(hot_grads, 'expert', scatter_dimension=2, tiled=True)  106 us
    all_to_all x1, waiting for transfers between devices, body(): lax.all_to_all(duplicate, 'expert', split_axis=1, concat_axis=1, tiled=True)  47.6 us
    add x14, other arithmetic, cycle_turn(): carried + fresh_terms[2]  35.6 us
    dot_general x16, matrix products, hot_terms(): jnp.einsum('ktu,td->kud', pre_grad, tokens, preferred_element_type=jnp.fl...  19.9 us
    dot_general x16, matrix products, hot_terms(): jnp.einsum('td,kud->ktu', tokens, weights[:2], preferred_element_type=jnp...  19.4 us
    ppermute x30, starting transfers between devices, passed_along(): return lax.ppermute(block, axis, route)  16.4 us
    slice x1, local copies, waits for them, and re-layouts, cold_terms(): row_block[0]  14.8 us
  transfers between devices with their start and end apart: 33, of which 32 were waited for; matrix products, arithmetic and copies ran while one was open for 17% of the time, Pallas kernels for 0%

commit v1 on v0

--- a/solution.py
+++ b/solution.py
@@ -89,7 +89,12 @@
     duplicate = jnp.broadcast_to(
         send_rows[:, :, None], (2, cold_count, 2, capacity, model_width)
     ).reshape(2, owner_count, capacity, model_width)
-    received = lax.all_to_all(duplicate, "expert", split_axis=1, concat_axis=1, tiled=True)
+    received = jnp.concatenate(
+        lax.all_to_all(
+            jnp.stack(jnp.split(duplicate, lax.axis_size("expert"), axis=1)), "expert", 0, 0
+        ),
+        axis=1,
+    )
     row_block = received.reshape(2, owner_count * capacity, model_width)
     out_part, dx_part, cold_grad_in, cold_grad_down = cold_terms(row_block, cold_in, cold_down)
     returned = lax.all_to_all(

time: 716 us -> 728 us (1.017)
  local copies, waits for them, and re-layouts: 57 us -> 67.9 us
    unnamed x38 -> x53, local copies, waits for them, and re-layouts: 1.92 us -> 13.6 us
where the time goes in v1:
time: 728 us; the launch traced here: 726 us
  waiting for transfers between devices  472 us (65%)
  matrix products  79.3 us (11%)
  local copies, waits for them, and re-layouts  67.9 us (9%)
  other arithmetic  57.8 us (8%)
  starting transfers between devices  32.7 us (4%)
  between operations  14.4 us (2%)
    ppermute x30, waiting for transfers between devices, passed_along(): return lax.ppermute(block, axis, route)  319 us
    reduce_scatter x1, waiting for transfers between devices, body(): lax.psum_scatter(hot_grads, 'expert', scatter_dimension=2, tiled=True)  106 us
    all_to_all x1, waiting for transfers between devices, body(): lax.all_to_all(jnp.stack(jnp.split(duplicate, lax.axis_size('expert'), ax...  47.6 us
    add x14, other arithmetic, cycle_turn(): carried + fresh_terms[2]  35.6 us
    dot_general x16, matrix products, hot_terms(): jnp.einsum('td,kud->ktu', tokens, weights[:2], preferred_element_type=jnp...  20.4 us
    dot_general x16, matrix products, hot_terms(): jnp.einsum('ktu,td->kud', pre_grad, tokens, preferred_element_type=jnp.fl...  18.7 us
    ppermute x30, starting transfers between devices, passed_along(): return lax.ppermute(block, axis, route)  17 us
    slice x1, local copies, waits for them, and re-layouts, cold_terms(): row_block[0]  14.8 us
  transfers between devices with their start and end apart: 33, of which 32 were waited for; matrix products, arithmetic and copies ran while one was open for 17% of the time, Pallas kernels for 0%

profile of v1, /device:TPU:8, one launch (start us, length us, event | category | flops | bytes accessed | tf_op | source)
XLA Modules:
  0.0 725.7 jit_solution(1243893202386198665)
XLA Ops:
  28.4 11.2 %all-to-all-start = ((bf16[16,2,1,20,2048]{4,1,3,2,0:T(2,128)(2,1)}), bf16[16,2,1,20,2048]{4,1,3,2,0:T(2,128)(2,1)}, u32[]{:S(2)}, u32[]{:S(2)}) async-start(bf16[16,2,1,20,2048]{4,1,3,2,0:T(2,128)(2,1)} %fusion.59), calls=%async_computation | async-start | bytes 5242880 | tf_op jit(solution)/shard_map/all_to_all | solution.py:93
  56.1 47.6 %all-to-all-done = bf16[16,2,1,20,2048]{4,1,3,2,0:T(2,128)(2,1)} async-done(((bf16[16,2,1,20,2048]{4,1,3,2,0:T(2,128)(2,1)}), bf16[16,2,1,20,2048]{4,1,3,2,0:T(2,128)(2,1)}, u32[]{:S(2)}, u32[]{:S(2)}) %all-to-all-start) | async-done | bytes 2621472 | tf_op jit(solution)/shard_map/all_to_all | solution.py:93
  103.7 14.8 %slice_reduce_fusion.1 = (bf16[16,20,2048]{2,1,0:T(8,128)(2,1)}, bf16[16,20,2048]{2,1,0:T(8,128)(2,1)}) fusion(bf16[2,16,1,20,2048]{4,0,3,2,1:T(2,128)(2,1)} %bitcast.55), kind=kLoop, calls=%fused_computation.49 | loop fusion | bytes 5242880 | tf_op jit(solution)/shard_map/slice | solution.py:44
  152.1 414.6 %while.16 = (s32[]{:T(128)}, bf16[3,44,2048]{2,1,0:T(8,128)(2,1)}, f32[3,44,2048]{2,1,0:T(8,128)}, f32[128,2048]{1,0:T(8,128)}, f32[128,2048]{1,0:T(8,128)}, /*i...) while((s32[]{:T(128)}, bf16[3,44,2048]{2,1,0:T(8,128)(2,1)}, ...), condition=%wide.region_1.2_spmd, body=%wide.region_0.0_spmd.sunk | while | flops 208863232 | bytes 40744796 | solution.py:140
  166.5 8.0 %collective-permute-done.1 = f32[3,44,2048]{2,1,0:T(8,128)} collective-permute-done((f32[3,44,2048]{2,1,0:T(8,128)}, f32[3,44,2048]{2,1,0:T(8,128)}, u32[]{:S(2)}, u32[]{:S(2)}) %collective-permute-start.1) | collective-permute-done | bytes 1081376 | tf_op jit(solution)/shard_map/while/body/eval_jaxpr/ppermute | solution.py:11
  191.4 8.0 %collective-permute-done.1 = f32[3,44,2048]{2,1,0:T(8,128)} collective-permute-done((f32[3,44,2048]{2,1,0:T(8,128)}, f32[3,44,2048]{2,1,0:T(8,128)}, u32[]{:S(2)}, u32[]{:S(2)}) %collective-permute-start.1) | collective-permute-done | bytes 1081376 | tf_op jit(solution)/shard_map/while/body/eval_jaxpr/ppermute | solution.py:11
  203.7 50.4 %collective-permute-done = bf16[3,44,2048]{2,1,0:T(8,128)(2,1)S(1)} collective-permute-done((bf16[3,44,2048]{2,1,0:T(8,128)(2,1)}, bf16[3,44,2048]{2,1,0:T(8,128)(2,1)S(1)}, u32[]{:S(2)}, u32[]{:S(2)}) %collective-permute-start) | collective-permute-done | bytes 540704 | tf_op jit(solution)/shard_map/while/body/eval_jaxpr/ppermute | solution.py:11
  270.5 10.7 %collective-permute-done = bf16[3,44,2048]{2,1,0:T(8,128)(2,1)S(1)} collective-permute-done((bf16[3,44,2048]{2,1,0:T(8,128)(2,1)}, bf16[3,44,2048]{2,1,0:T(8,128)(2,1)S(1)}, u32[]{:S(2)}, u32[]{:S(2)}) %collective-permute-start) | collective-permute-done | bytes 540704 | tf_op jit(solution)/shard_map/while/body/eval_jaxpr/ppermute | solution.py:11
  297.5 10.7 %collective-permute-done = bf16[3,44,2048]{2,1,0:T(8,128)(2,1)S(1)} collective-permute-done((bf16[3,44,2048]{2,1,0:T(8,128)(2,1)}, bf16[3,44,2048]{2,1,0:T(8,128)(2,1)S(1)}, u32[]{:S(2)}, u32[]{:S(2)}) %collective-permute-start) | collective-permute-done | bytes 540704 | tf_op jit(solution)/shard_map/while/body/eval_jaxpr/ppermute | solution.py:11
  324.6 10.7 %collective-permute-done = bf16[3,44,2048]{2,1,0:T(8,128)(2,1)S(1)} collective-permute-done((bf16[3,44,2048]{2,1,0:T(8,128)(2,1)}, bf16[3,44,2048]{2,1,0:T(8,128)(2,1)S(1)}, u32[]{:S(2)}, u32[]{:S(2)}) %collective-permute-start) | collective-permute-done | bytes 540704 | tf_op jit(solution)/shard_map/while/body/eval_jaxpr/ppermute | solution.py:11
  340.0 8.0 %collective-permute-done.1 = f32[3,44,2048]{2,1,0:T(8,128)} collective-permute-done((f32[3,44,2048]{2,1,0:T(8,128)}, f32[3,44,2048]{2,1,0:T(8,128)}, u32[]{:S(2)}, u32[]{:S(2)}) %collective-permute-start.1) | collective-permute-done | bytes 1081376 | tf_op jit(solution)/shard_map/while/body/eval_jaxpr/ppermute | solution.py:11
  351.6 10.7 %collective-permute-done = bf16[3,44,2048]{2,1,0:T(8,128)(2,1)S(1)} collective-permute-done((bf16[3,44,2048]{2,1,0:T(8,128)(2,1)}, bf16[3,44,2048]{2,1,0:T(8,128)(2,1)S(1)}, u32[]{:S(2)}, u32[]{:S(2)}) %collective-permute-start) | collective-permute-done | bytes 540704 | tf_op jit(solution)/shard_map/while/body/eval_jaxpr/ppermute | solution.py:11
  367.0 8.0 %collective-permute-done.1 = f32[3,44,2048]{2,1,0:T(8,128)} collective-permute-done((f32[3,44,2048]{2,1,0:T(8,128)}, f32[3,44,2048]{2,1,0:T(8,128)}, u32[]{:S(2)}, u32[]{:S(2)}) %collective-permute-start.1) | collective-permute-done | bytes 1081376 | tf_op jit(solution)/shard_map/while/body/eval_jaxpr/ppermute | solution.py:11
  378.6 10.7 %collective-permute-done = bf16[3,44,2048]{2,1,0:T(8,128)(2,1)S(1)} collective-permute-done((bf16[3,44,2048]{2,1,0:T(8,128)(2,1)}, bf16[3,44,2048]{2,1,0:T(8,128)(2,1)S(1)}, u32[]{:S(2)}, u32[]{:S(2)}) %collective-permute-start) | collective-permute-done | bytes 540704 | tf_op jit(solution)/shard_map/while/body/eval_jaxpr/ppermute | solution.py:11
  394.0 8.0 %collective-permute-done.1 = f32[3,44,2048]{2,1,0:T(8,128)} collective-permute-done((f32[3,44,2048]{2,1,0:T(8,128)}, f32[3,44,2048]{2,1,0:T(8,128)}, u32[]{:S(2)}, u32[]{:S(2)}) %collective-permute-start.1) | collective-permute-done | bytes 1081376 | tf_op jit(solution)/shard_map/while/body/eval_jaxpr/ppermute | solution.py:11
  405.6 10.7 %collective-permute-done = bf16[3,44,2048]{2,1,0:T(8,128)(2,1)S(1)} collective-permute-done((bf16[3,44,2048]{2,1,0:T(8,128)(2,1)}, bf16[3,44,2048]{2,1,0:T(8,128)(2,1)S(1)}, u32[]{:S(2)}, u32[]{:S(2)}) %collective-permute-start) | collective-permute-done | bytes 540704 | tf_op jit(solution)/shard_map/while/body/eval_jaxpr/ppermute | solution.py:11
  421.0 8.0 %collective-permute-done.1 = f32[3,44,2048]{2,1,0:T(8,128)} collective-permute-done((f32[3,44,2048]{2,1,0:T(8,128)}, f32[3,44,2048]{2,1,0:T(8,128)}, u32[]{:S(2)}, u32[]{:S(2)}) %collective-permute-start.1) | collective-permute-done | bytes 1081376 | tf_op jit(solution)/shard_map/while/body/eval_jaxpr/ppermute | solution.py:11
  432.6 10.7 %collective-permute-done = bf16[3,44,2048]{2,1,0:T(8,128)(2,1)S(1)} collective-permute-done((bf16[3,44,2048]{2,1,0:T(8,128)(2,1)}, bf16[3,44,2048]{2,1,0:T(8,128)(2,1)S(1)}, u32[]{:S(2)}, u32[]{:S(2)}) %collective-permute-start) | collective-permute-done | bytes 540704 | tf_op jit(solution)/shard_map/while/body/eval_jaxpr/ppermute | solution.py:11
  459.7 10.7 %collective-permute-done = bf16[3,44,2048]{2,1,0:T(8,128)(2,1)S(1)} collective-permute-done((bf16[3,44,2048]{2,1,0:T(8,128)(2,1)}, bf16[3,44,2048]{2,1,0:T(8,128)(2,1)S(1)}, u32[]{:S(2)}, u32[]{:S(2)}) %collective-permute-start) | collective-permute-done | bytes 540704 | tf_op jit(solution)/shard_map/while/body/eval_jaxpr/ppermute | solution.py:11
  486.7 10.7 %collective-permute-done = bf16[3,44,2048]{2,1,0:T(8,128)(2,1)S(1)} collective-permute-done((bf16[3,44,2048]{2,1,0:T(8,128)(2,1)}, bf16[3,44,2048]{2,1,0:T(8,128)(2,1)S(1)}, u32[]{:S(2)}, u32[]{:S(2)}) %collective-permute-start) | collective-permute-done | bytes 540704 | tf_op jit(solution)/shard_map/while/body/eval_jaxpr/ppermute | solution.py:11
  513.7 10.7 %collective-permute-done = bf16[3,44,2048]{2,1,0:T(8,128)(2,1)S(1)} collective-permute-done((bf16[3,44,2048]{2,1,0:T(8,128)(2,1)}, bf16[3,44,2048]{2,1,0:T(8,128)(2,1)S(1)}, u32[]{:S(2)}, u32[]{:S(2)}) %collective-permute-start) | collective-permute-done | bytes 540704 | tf_op jit(solution)/shard_map/while/body/eval_jaxpr/ppermute | solution.py:11
  540.7 10.7 %collective-permute-done = bf16[3,44,2048]{2,1,0:T(8,128)(2,1)S(1)} collective-permute-done((bf16[3,44,2048]{2,1,0:T(8,128)(2,1)}, bf16[3,44,2048]{2,1,0:T(8,128)(2,1)S(1)}, u32[]{:S(2)}, u32[]{:S(2)}) %collective-permute-start) | collective-permute-done | bytes 540704 | tf_op jit(solution)/shard_map/while/body/eval_jaxpr/ppermute | solution.py:11
  568.6 16.4 %collective-permute-done.3 = f32[3,44,2048]{2,1,0:T(8,128)S(1)} collective-permute-done((f32[3,44,2048]{2,1,0:T(8,128)}, f32[3,44,2048]{2,1,0:T(8,128)S(1)}, u32[]{:S(2)}, u32[]{:S(2)}) %collective-permute-start.3) | collective-permute-done | bytes 1081376 | tf_op jit(solution)/shard_map/ppermute | solution.py:11
  586.2 105.7 %reduce-scatter.2.cloned.1.call-done = f32[3,44,128]{2,1,0:T(8,128)} async-done(((f32[3,44,2048]{2,1,0:T(8,128)}), f32[3,44,128]{2,1,0:T(8,128)}) %reduce-scatter.2.cloned.1.call-update) | async-done | bytes 67600 | tf_op jit(solution)/shard_map/reduce_scatter | solution.py:143
  (424 shorter events, 298.3 us)
Async XLA Ops:
  28.4 75.3 %all-to-all-start = ((bf16[16,2,1,20,2048]{4,1,3,2,0:T(2,128)(2,1)}), bf16[16,2,1,20,2048]{4,1,3,2,0:T(2,128)(2,1)}, u32[]{:S(2)}, u32[]{:S(2)}) async-start(bf16[16,2,1,20,2048]{4,1,3,2,0:T(2,128)(2,1)} %fusion.59), calls=%async_computation | async-start | bytes 5242880 | tf_op jit(solution)/shard_map/all_to_all | solution.py:93
  147.6 553.5 %all-to-all-start.1 = ((bf16[2,16,20,2048]{3,0,2,1:T(2,128)(2,1)}), bf16[2,16,20,2048]{3,0,2,1:T(2,128)(2,1)}, u32[]{:S(2)}, u32[]{:S(2)}) async-start(bf16[2,16,20,2048]{3,0,2,1:T(2,128)(2,1)} %copy.62), calls=%async_computation.1 | async-start | bytes 5242880 | tf_op jit(solution)/shard_map/all_to_all | solution.py:100
  152.1 539.8 %reduce-scatter.2.cloned.1.call-start = ((), (), s32[]{:S(2)}) async-start(), calls=%async_computation.3 | async-start | bytes 1253376 | tf_op jit(solution)/shard_map/reduce_scatter | solution.py:143
  152.2 22.3 %collective-permute-start.1 = (f32[3,44,2048]{2,1,0:T(8,128)}, f32[3,44,2048]{2,1,0:T(8,128)}, u32[]{:S(2)}, u32[]{:S(2)}) collective-permute-start(f32[3,44,2048]{2,1,0:T(8,128)} %get-tuple-element.166), channel_id=1, source_target_pairs={{240,0},{0,16},{16,32},{32,48},{48,64},{64,80},{80,96},{96,112},{1... | collective-permute-start | bytes 3244040 | tf_op jit(solution)/shard_map/while/body/eval_jaxpr/ppermute | solution.py:11
  177.1 22.3 %collective-permute-start.1 = (f32[3,44,2048]{2,1,0:T(8,128)}, f32[3,44,2048]{2,1,0:T(8,128)}, u32[]{:S(2)}, u32[]{:S(2)}) collective-permute-start(f32[3,44,2048]{2,1,0:T(8,128)} %get-tuple-element.166), channel_id=1, source_target_pairs={{240,0},{0,16},{16,32},{32,48},{48,64},{64,80},{80,96},{96,112},{1... | collective-permute-start | bytes 3244040 | tf_op jit(solution)/shard_map/while/body/eval_jaxpr/ppermute | solution.py:11
  202.0 52.2 %collective-permute-start = (bf16[3,44,2048]{2,1,0:T(8,128)(2,1)}, bf16[3,44,2048]{2,1,0:T(8,128)(2,1)S(1)}, u32[]{:S(2)}, u32[]{:S(2)}) collective-permute-start(bf16[3,44,2048]{2,1,0:T(8,128)(2,1)} %get-tuple-element.165), channel_id=1, source_target_pairs={{240,0},{0,16},{16,32},{32,48},{48,64},{64,80},{80,96},{96,112},{1... | collective-permute-start | bytes 1622024 | tf_op jit(solution)/shard_map/while/body/eval_jaxpr/ppermute | solution.py:11
  202.1 64.8 %collective-permute-start.1 = (f32[3,44,2048]{2,1,0:T(8,128)}, f32[3,44,2048]{2,1,0:T(8,128)}, u32[]{:S(2)}, u32[]{:S(2)}) collective-permute-start(f32[3,44,2048]{2,1,0:T(8,128)} %get-tuple-element.166), channel_id=1, source_target_pairs={{240,0},{0,16},{16,32},{32,48},{48,64},{64,80},{80,96},{96,112},{1... | collective-permute-start | bytes 3244040 | tf_op jit(solution)/shard_map/while/body/eval_jaxpr/ppermute | solution.py:11
  269.5 11.7 %collective-permute-start = (bf16[3,44,2048]{2,1,0:T(8,128)(2,1)}, bf16[3,44,2048]{2,1,0:T(8,128)(2,1)S(1)}, u32[]{:S(2)}, u32[]{:S(2)}) collective-permute-start(bf16[3,44,2048]{2,1,0:T(8,128)(2,1)} %get-tuple-element.165), channel_id=1, source_target_pairs={{240,0},{0,16},{16,32},{32,48},{48,64},{64,80},{80,96},{96,112},{1... | collective-permute-start | bytes 1622024 | tf_op jit(solution)/shard_map/while/body/eval_jaxpr/ppermute | solution.py:11
  269.6 24.4 %collective-permute-start.1 = (f32[3,44,2048]{2,1,0:T(8,128)}, f32[3,44,2048]{2,1,0:T(8,128)}, u32[]{:S(2)}, u32[]{:S(2)}) collective-permute-start(f32[3,44,2048]{2,1,0:T(8,128)} %get-tuple-element.166), channel_id=1, source_target_pairs={{240,0},{0,16},{16,32},{32,48},{48,64},{64,80},{80,96},{96,112},{1... | collective-permute-start | bytes 3244040 | tf_op jit(solution)/shard_map/while/body/eval_jaxpr/ppermute | solution.py:11
  296.5 11.7 %collective-permute-start = (bf16[3,44,2048]{2,1,0:T(8,128)(2,1)}, bf16[3,44,2048]{2,1,0:T(8,128)(2,1)S(1)}, u32[]{:S(2)}, u32[]{:S(2)}) collective-permute-start(bf16[3,44,2048]{2,1,0:T(8,128)(2,1)} %get-tuple-element.165), channel_id=1, source_target_pairs={{240,0},{0,16},{16,32},{32,48},{48,64},{64,80},{80,96},{96,112},{1... | collective-permute-start | bytes 1622024 | tf_op jit(solution)/shard_map/while/body/eval_jaxpr/ppermute | solution.py:11
  296.6 24.4 %collective-permute-start.1 = (f32[3,44,2048]{2,1,0:T(8,128)}, f32[3,44,2048]{2,1,0:T(8,128)}, u32[]{:S(2)}, u32[]{:S(2)}) collective-permute-start(f32[3,44,2048]{2,1,0:T(8,128)} %get-tuple-element.166), channel_id=1, source_target_pairs={{240,0},{0,16},{16,32},{32,48},{48,64},{64,80},{80,96},{96,112},{1... | collective-permute-start | bytes 3244040 | tf_op jit(solution)/shard_map/while/body/eval_jaxpr/ppermute | solution.py:11
  323.5 11.7 %collective-permute-start = (bf16[3,44,2048]{2,1,0:T(8,128)(2,1)}, bf16[3,44,2048]{2,1,0:T(8,128)(2,1)S(1)}, u32[]{:S(2)}, u32[]{:S(2)}) collective-permute-start(bf16[3,44,2048]{2,1,0:T(8,128)(2,1)} %get-tuple-element.165), channel_id=1, source_target_pairs={{240,0},{0,16},{16,32},{32,48},{48,64},{64,80},{80,96},{96,112},{1... | collective-permute-start | bytes 1622024 | tf_op jit(solution)/shard_map/while/body/eval_jaxpr/ppermute | solution.py:11
  323.6 24.4 %collective-permute-start.1 = (f32[3,44,2048]{2,1,0:T(8,128)}, f32[3,44,2048]{2,1,0:T(8,128)}, u32[]{:S(2)}, u32[]{:S(2)}) collective-permute-start(f32[3,44,2048]{2,1,0:T(8,128)} %get-tuple-element.166), channel_id=1, source_target_pairs={{240,0},{0,16},{16,32},{32,48},{48,64},{64,80},{80,96},{96,112},{1... | collective-permute-start | bytes 3244040 | tf_op jit(solution)/shard_map/while/body/eval_jaxpr/ppermute | solution.py:11
  350.5 11.7 %collective-permute-start = (bf16[3,44,2048]{2,1,0:T(8,128)(2,1)}, bf16[3,44,2048]{2,1,0:T(8,128)(2,1)S(1)}, u32[]{:S(2)}, u32[]{:S(2)}) collective-permute-start(bf16[3,44,2048]{2,1,0:T(8,128)(2,1)} %get-tuple-element.165), channel_id=1, source_target_pairs={{240,0},{0,16},{16,32},{32,48},{48,64},{64,80},{80,96},{96,112},{1... | collective-permute-start | bytes 1622024 | tf_op jit(solution)/shard_map/while/body/eval_jaxpr/ppermute | solution.py:11
  350.6 24.4 %collective-permute-start.1 = (f32[3,44,2048]{2,1,0:T(8,128)}, f32[3,44,2048]{2,1,0:T(8,128)}, u32[]{:S(2)}, u32[]{:S(2)}) collective-permute-start(f32[3,44,2048]{2,1,0:T(8,128)} %get-tuple-element.166), channel_id=1, source_target_pairs={{240,0},{0,16},{16,32},{32,48},{48,64},{64,80},{80,96},{96,112},{1... | collective-permute-start | bytes 3244040 | tf_op jit(solution)/shard_map/while/body/eval_jaxpr/ppermute | solution.py:11
  377.6 24.4 %collective-permute-start.1 = (f32[3,44,2048]{2,1,0:T(8,128)}, f32[3,44,2048]{2,1,0:T(8,128)}, u32[]{:S(2)}, u32[]{:S(2)}) collective-permute-start(f32[3,44,2048]{2,1,0:T(8,128)} %get-tuple-element.166), channel_id=1, source_target_pairs={{240,0},{0,16},{16,32},{32,48},{48,64},{64,80},{80,96},{96,112},{1... | collective-permute-start | bytes 3244040 | tf_op jit(solution)/shard_map/while/body/eval_jaxpr/ppermute | solution.py:11
  404.7 24.4 %collective-permute-start.1 = (f32[3,44,2048]{2,1,0:T(8,128)}, f32[3,44,2048]{2,1,0:T(8,128)}, u32[]{:S(2)}, u32[]{:S(2)}) collective-permute-start(f32[3,44,2048]{2,1,0:T(8,128)} %get-tuple-element.166), channel_id=1, source_target_pairs={{240,0},{0,16},{16,32},{32,48},{48,64},{64,80},{80,96},{96,112},{1... | collective-permute-start | bytes 3244040 | tf_op jit(solution)/shard_map/while/body/eval_jaxpr/ppermute | solution.py:11
  431.7 24.4 %collective-permute-start.1 = (f32[3,44,2048]{2,1,0:T(8,128)}, f32[3,44,2048]{2,1,0:T(8,128)}, u32[]{:S(2)}, u32[]{:S(2)}) collective-permute-start(f32[3,44,2048]{2,1,0:T(8,128)} %get-tuple-element.166), channel_id=1, source_target_pairs={{240,0},{0,16},{16,32},{32,48},{48,64},{64,80},{80,96},{96,112},{1... | collective-permute-start | bytes 3244040 | tf_op jit(solution)/shard_map/while/body/eval_jaxpr/ppermute | solution.py:11
  458.7 24.4 %collective-permute-start.1 = (f32[3,44,2048]{2,1,0:T(8,128)}, f32[3,44,2048]{2,1,0:T(8,128)}, u32[]{:S(2)}, u32[]{:S(2)}) collective-permute-start(f32[3,44,2048]{2,1,0:T(8,128)} %get-tuple-element.166), channel_id=1, source_target_pairs={{240,0},{0,16},{16,32},{32,48},{48,64},{64,80},{80,96},{96,112},{1... | collective-permute-start | bytes 3244040 | tf_op jit(solution)/shard_map/while/body/eval_jaxpr/ppermute | solution.py:11
  485.7 24.4 %collective-permute-start.1 = (f32[3,44,2048]{2,1,0:T(8,128)}, f32[3,44,2048]{2,1,0:T(8,128)}, u32[]{:S(2)}, u32[]{:S(2)}) collective-permute-start(f32[3,44,2048]{2,1,0:T(8,128)} %get-tuple-element.166), channel_id=1, source_target_pairs={{240,0},{0,16},{16,32},{32,48},{48,64},{64,80},{80,96},{96,112},{1... | collective-permute-start | bytes 3244040 | tf_op jit(solution)/shard_map/while/body/eval_jaxpr/ppermute | solution.py:11
  512.7 11.7 %collective-permute-start = (bf16[3,44,2048]{2,1,0:T(8,128)(2,1)}, bf16[3,44,2048]{2,1,0:T(8,128)(2,1)S(1)}, u32[]{:S(2)}, u32[]{:S(2)}) collective-permute-start(bf16[3,44,2048]{2,1,0:T(8,128)(2,1)} %get-tuple-element.165), channel_id=1, source_target_pairs={{240,0},{0,16},{16,32},{32,48},{48,64},{64,80},{80,96},{96,112},{1... | collective-permute-start | bytes 1622024 | tf_op jit(solution)/shard_map/while/body/eval_jaxpr/ppermute | solution.py:11
  512.8 24.4 %collective-permute-start.1 = (f32[3,44,2048]{2,1,0:T(8,128)}, f32[3,44,2048]{2,1,0:T(8,128)}, u32[]{:S(2)}, u32[]{:S(2)}) collective-permute-start(f32[3,44,2048]{2,1,0:T(8,128)} %get-tuple-element.166), channel_id=1, source_target_pairs={{240,0},{0,16},{16,32},{32,48},{48,64},{64,80},{80,96},{96,112},{1... | collective-permute-start | bytes 3244040 | tf_op jit(solution)/shard_map/while/body/eval_jaxpr/ppermute | solution.py:11
  539.8 24.4 %collective-permute-start.1 = (f32[3,44,2048]{2,1,0:T(8,128)}, f32[3,44,2048]{2,1,0:T(8,128)}, u32[]{:S(2)}, u32[]{:S(2)}) collective-permute-start(f32[3,44,2048]{2,1,0:T(8,128)} %get-tuple-element.166), channel_id=1, source_target_pairs={{240,0},{0,16},{16,32},{32,48},{48,64},{64,80},{80,96},{96,112},{1... | collective-permute-start | bytes 3244040 | tf_op jit(solution)/shard_map/while/body/eval_jaxpr/ppermute | solution.py:11
  566.7 18.2 %collective-permute-start.3 = (f32[3,44,2048]{2,1,0:T(8,128)}, f32[3,44,2048]{2,1,0:T(8,128)S(1)}, u32[]{:S(2)}, u32[]{:S(2)}) collective-permute-start(f32[3,44,2048]{2,1,0:T(8,128)} %get-tuple-element.186), channel_id=1, source_target_pairs={{240,0},{0,16},{16,32},{32,48},{48,64},{64,80},{80,96},{96,112},{1... | collective-permute-start | bytes 3244040 | tf_op jit(solution)/shard_map/ppermute | solution.py:11
  (111 other events, 1249.9 us)
Sparse Core Ops, SparseCore 0:
  586.3 105.5 reduce-scatter.1
